TPU v7x, 256 devices: a whole 4x4x8 slice. The times are simulated.
256 devices in a mesh: seq: 128 (over z, y, x_lo, core), dp: 2 (over x_hi).
Axes of the slice: x: 4 (x_hi: 2, x_lo: 2; x = x_hi * 2 + x_lo), y: 4, z: 8, core: 2. Of those that a mesh axis runs over, the one named last changes fastest.
Arguments:
- frames: bfloat16 [2, 16384, 1024], P('dp', 'seq'), may hold values from -36 to 36
- kernel: bfloat16 [31, 1024], replicated, may hold values from -1 to 1
- norm_gain: float32 [1024], replicated, may hold values from 0.5 to 1.5
- router: bfloat16 [1024, 32], replicated, may hold values from -0.1875 to 0.1875
- experts: int32 [2, 16384, 2], P('dp', 'seq'), may hold values from 0 to 31, all different within a row; in each aligned block of 128 rows (0 to 127, 128 to 255, ..., all dimensions but the last counted through in order) at most 16 rows name the same one
- w_in: bfloat16 [128, 1024, 512], P('seq'), may hold values from -0.1875 to 0.1875
- w_out: bfloat16 [128, 512, 1024], P('seq'), may hold values from -0.125 to 0.125
- cotangent: bfloat16 [2, 16384, 1024], P('dp', 'seq'), may hold values from -8 to 8
Outputs:
- mixed: bfloat16 [2, 16384, 1024], P('dp', 'seq')
- grad_frames: bfloat16 [2, 16384, 1024], P('dp', 'seq')
- grad_kernel: float32 [31, 1024], replicated
- grad_gain: float32 [1024], replicated
- grad_router: float32 [1024, 32], replicated
- grad_w_in: float32 [128, 1024, 512], P('seq')
- grad_w_out: float32 [128, 512, 1024], P('seq')
Inputs may be any that keep to these rules, and one draw needn't show every extreme that they name: Each frame names 2 different experts; in each aligned block of 128 frames no expert is named more than 16 times, a bound that some block reaches.
All inputs are finite; a program needn't handle non-finite values.
Results may differ from a plain program's by a relative error of at most 0.0075.
Values may be sent and summed in bfloat16 or wider, within the bound.
No kernel may reach another device: no remote copies, remote signals or barrier semaphores. Data moves between devices by JAX's collectives and lax.ppermute only.
A program may use at most 128 MiB of HBM per device.

v0:
```python
import jax
import jax.numpy as jnp
from jax import lax
from jax.sharding import Mesh
from jax.sharding import PartitionSpec as P

eps = 1e-06
SEQ = ("z", "y", "xl", "c")
GRP = ("z", "y")


def padded_2(shard, axis, size, width):
    length = shard.shape[0]
    up = [(i, (i + 1) % size) for i in range(size - 1)]
    down = [(j, i) for i, j in up]
    last = lax.slice_in_dim(shard, length - width, length, axis=0)
    initial = lax.slice_in_dim(shard, 0, width, axis=0)
    before = lax.ppermute(last, axis, up)
    after = lax.ppermute(initial, axis, down)
    return jnp.concatenate([before, shard, after], axis=0)


def conv_forward(padded, kernel, row_count):
    summed = jnp.zeros((row_count, padded.shape[1]), jnp.float32)
    for offset in range(kernel.shape[0]):
        summed = summed + kernel[offset].astype(jnp.float32) * padded[
            offset : offset + row_count
        ].astype(jnp.float32)
    return summed


def conv_transpose(padded, kernel, row_count):
    length = kernel.shape[0]
    summed = jnp.zeros((row_count, padded.shape[1]), jnp.float32)
    for offset in range(length):
        start = length - 1 - offset
        summed = summed + kernel[offset].astype(jnp.float32) * padded[start : start + row_count]
    return summed


def kernel_terms(padded, upstream, length, row_count):
    return jnp.stack(
        [
            jnp.sum(padded[offset : offset + row_count].astype(jnp.float32) * upstream, axis=0)
            for offset in range(length)
        ]
    )


def normalize(summed, norm_gain):
    square = jnp.mean(summed * summed, axis=-1, keepdims=True)
    return summed * lax.rsqrt(square + eps) * norm_gain


def slot_numbers(expert_ids, expert_count):
    onehot = (expert_ids[:, None] == jnp.arange(expert_count, dtype=jnp.int32)[None, :]).astype(
        jnp.int32
    )
    ranks = jnp.cumsum(onehot, axis=0) - onehot
    return jnp.sum(ranks * onehot, axis=1)


def gate_values(normed_b, router, first_ids, second_ids):
    logits = jnp.dot(normed_b, router, preferred_element_type=jnp.float32)
    columns = jnp.arange(router.shape[1], dtype=jnp.int32)[None, :]
    pick_diff = (first_ids[:, None] == columns).astype(jnp.float32) - (
        second_ids[:, None] == columns
    ).astype(jnp.float32)
    gate_one = jax.nn.sigmoid(jnp.sum(logits * pick_diff, axis=1))
    return (gate_one, 1.0 - gate_one, pick_diff)


def swish_parts(pre_act):
    squash = jax.nn.sigmoid(pre_act)
    return (pre_act * squash, squash * (1.0 + pre_act * (1.0 - squash)))


def gate_backward(upstream, out_one, out_two, gate_one, gate_two, pick_diff, normed_b, router):
    grad_gap = (
        (jnp.sum(upstream * out_one, axis=1) - jnp.sum(upstream * out_two, axis=1))
        * gate_one
        * gate_two
    )
    grad_logits = (grad_gap[:, None] * pick_diff).astype(jnp.bfloat16)
    router_term = jnp.dot(normed_b.T, grad_logits, preferred_element_type=jnp.float32)
    normed_term = jnp.dot(grad_logits, router.T, preferred_element_type=jnp.float32)
    return (router_term, normed_term)


def body(frames, kernel, norm_gain, router, experts, w_in, w_out, cotangent):
    inputs_dev = frames[0]
    row_count = inputs_dev.shape[0]
    width = inputs_dev.shape[1]
    length = kernel.shape[0]
    half_width = length // 2
    expert_count = router.shape[1]
    top_count = experts.shape[2]
    capacity = 2 * row_count * top_count // expert_count
    seq_size = lax.psum(1, SEQ)
    in_weights = w_in[0]
    out_weights = w_out[0]
    padded = padded_2(inputs_dev, SEQ, seq_size, half_width)
    summed = inputs_dev.astype(jnp.float32) + conv_forward(padded, kernel, row_count)
    normed_b = normalize(summed, norm_gain).astype(jnp.bfloat16)
    choice_ids = experts[0]
    gate_one, gate_two, pick_diff = gate_values(
        normed_b, router, choice_ids[:, 0], choice_ids[:, 1]
    )
    flat_ids = choice_ids.reshape(-1)
    slot_index = slot_numbers(flat_ids, expert_count)
    position = flat_ids * capacity + slot_index
    dispatch_table = (
        lax.broadcasted_iota(jnp.int32, (expert_count * capacity, flat_ids.shape[0]), 0)
        == position[None, :]
    ).astype(jnp.bfloat16)
    upstream = cotangent[0].astype(jnp.float32)
    repeated = jnp.repeat(normed_b, top_count, axis=0)
    grad_assigned = jnp.stack([gate_one[:, None] * upstream, gate_two[:, None] * upstream], axis=1)
    grad_values = grad_assigned.reshape(row_count * top_count, width).astype(jnp.bfloat16)
    both = jnp.concatenate([repeated, grad_values], axis=1)
    packed = jnp.dot(dispatch_table, both, preferred_element_type=jnp.float32).astype(jnp.bfloat16)
    packed = packed.reshape(expert_count, capacity, 2 * width)
    arrived = lax.all_to_all(packed, GRP, split_axis=0, concat_axis=0, tiled=True)
    arrived = lax.all_gather(arrived, "xl", axis=0, tiled=False)
    arrived = lax.all_gather(arrived, "c", axis=0, tiled=False)
    rows_shape = arrived.shape
    flat = arrived.reshape(-1, 2 * width)
    flat_rows = flat[:, :width]
    flat_grads = flat[:, width:]
    pre_act = jnp.dot(flat_rows, in_weights, preferred_element_type=jnp.float32)
    hidden_f, slope = swish_parts(pre_act)
    hidden = hidden_f.astype(jnp.bfloat16)
    partial_rows = jnp.dot(hidden, out_weights, preferred_element_type=jnp.float32).astype(
        jnp.bfloat16
    )
    grad_hidden = jnp.dot(flat_grads, out_weights.T, preferred_element_type=jnp.float32)
    grad_pre = (grad_hidden * slope).astype(jnp.bfloat16)
    out_term = jnp.dot(hidden.T, flat_grads, preferred_element_type=jnp.float32)
    in_term = jnp.dot(flat_rows.T, grad_pre, preferred_element_type=jnp.float32)
    grad_part = jnp.dot(grad_pre, in_weights.T, preferred_element_type=jnp.float32).astype(
        jnp.bfloat16
    )
    dp_pair = [(0, 1), (1, 0)]
    in_mine, out_mine = (in_term.astype(jnp.bfloat16), out_term.astype(jnp.bfloat16))
    in_other = lax.ppermute(in_mine, "dp", dp_pair)
    out_other = lax.ppermute(out_mine, "dp", dp_pair)
    dp_first = lax.axis_index("dp") == 0
    in_a = jnp.where(dp_first, in_mine, in_other).astype(jnp.float32)
    in_b = jnp.where(dp_first, in_other, in_mine).astype(jnp.float32)
    out_a = jnp.where(dp_first, out_mine, out_other).astype(jnp.float32)
    out_b = jnp.where(dp_first, out_other, out_mine).astype(jnp.float32)
    grad_in = in_a + in_b
    grad_out = out_a + out_b
    back = jnp.concatenate([partial_rows, grad_part], axis=1).reshape(rows_shape)
    back = lax.psum_scatter(back, "c", scatter_dimension=0, tiled=True)
    back = lax.psum_scatter(back, "xl", scatter_dimension=1, tiled=True)
    back = back.reshape(expert_count, capacity, 2 * width)
    totals = lax.all_to_all(back, GRP, split_axis=0, concat_axis=0, tiled=True)
    totals = totals.reshape(expert_count * capacity, 2 * width)
    picked = jnp.take(totals, position, axis=0).astype(jnp.float32)
    picked = picked.reshape(row_count, top_count, 2 * width)
    out_one = picked[:, 0, :width]
    out_two = picked[:, 1, :width]
    normed_grads = picked[:, 0, width:] + picked[:, 1, width:]
    mixed = (summed + gate_one[:, None] * out_one + gate_two[:, None] * out_two).astype(
        jnp.bfloat16
    )
    router_term, normed_term = gate_backward(
        upstream, out_one, out_two, gate_one, gate_two, pick_diff, normed_b, router
    )
    pullback = jax.vjp(normalize, summed, norm_gain)[1]
    summed_grad, gain_term = pullback(normed_grads + normed_term)
    upstream_total = upstream + summed_grad
    padded_grad = padded_2(upstream_total.astype(jnp.bfloat16), SEQ, seq_size, half_width).astype(
        upstream_total.dtype
    )
    grad_frames = (upstream_total + conv_transpose(padded_grad, kernel, row_count)).astype(
        jnp.bfloat16
    )
    kernel_term = kernel_terms(padded, upstream_total, length, row_count)
    small = jnp.concatenate([kernel_term, gain_term[None, :], router_term.T], axis=0)
    for axis in ("c", "xl", "y", "z", "dp"):
        small = lax.psum(small, axis)
    grad_kernel = small[:length]
    grad_gain = small[length]
    grad_router = small[length + 1 :].T
    return (
        mixed[None],
        grad_frames[None],
        grad_kernel,
        grad_gain,
        grad_router,
        grad_in[None],
        grad_out[None],
    )


def solution(mesh):
    split_mesh = Mesh(mesh.devices.reshape(8, 4, 2, 2, 2), SEQ + ("dp",))
    return jax.shard_map(
        body,
        mesh=split_mesh,
        in_specs=(
            P("dp", SEQ, None),
            P(),
            P(),
            P(),
            P("dp", SEQ, None),
            P(SEQ, None, None),
            P(SEQ, None, None),
            P("dp", SEQ, None),
        ),
        out_specs=(
            P("dp", SEQ, None),
            P("dp", SEQ, None),
            P(),
            P(),
            P(),
            P(SEQ, None, None),
            P(SEQ, None, None),
        ),
        check_vma=False,
    )
```

profile of v0, /device:TPU:1, one launch (start us, length us, event | category | flops | bytes accessed | tf_op | source)
XLA Modules:
  0.0 620.3 jit_solution(765407525963802871)
XLA Ops:
  7.2 0.9 slice_bitcast_fusion.4
  8.1 4.5 collective-permute-start
  12.6 1.9 collective-permute-start.1
  14.6 0.8 copy.43
  15.6 1.0 slice_convert_fusion.29
  16.7 1.2 slice_convert_fusion.30
  18.9 0.8 slice_bitcast_fusion.6
  19.7 9.2 %multiply_reduce_fusion.2 = (f32[128]{0:T(128)S(1)}, f32[128,1024]{1,0:T(8,128)S(1)}) fusion(bf16[15,1024]{1,0:T(8,128)(2,1)S(1)} %collective-permute-done.1, bf16[128,1024]{1,0:T(8,128)(2,1)} %bitcast.175, f32[1024]{0:T(1024)S(1)} %bitcast.202, f32[1024]{0:T(1024)S(1)} %bitcast.204, f32[1024]{0:T(1024)S(1)} %bitcast.208, f32[1024]{0:T(1024)S(1)} %bitcast.210, ...), kind=kLoop, calls=%fused_computation.269 | loop fusion | flops 24248192 | bytes 975360 | tf_op jit(solution)/shard_map/reduce_sum | solution.py:51
  29.8 0.8 multiply_convert_fusion.2
  30.6 1.0 fusion.16
  33.2 0.7 convolution_convert_fusion.2
  33.9 58.0 %all_to_all.10 = bf16[32,16,2048]{2,1,0:T(8,128)(2,1)} all-to-all(bf16[32,16,2048]{2,1,0:T(8,128)(2,1)S(1)} %bitcast.174), channel_id=1, replica_groups=mesh['z'=8,'y'=4,'xl'=2,'c'=2,'dp'=2] {'z','y'}, dimensions={0} | all-to-all | bytes 4194304 | tf_op jit(solution)/shard_map/all_to_all | solution.py:123
  92.0 63.6 %all-gather.5.cloned.1.call-done = bf16[64,16,2048]{2,1,0:T(8,128)(2,1)} async-done(((bf16[32,16,2048]{2,1,0:T(8,128)(2,1)}), bf16[64,16,2048]{2,1,0:T(8,128)(2,1)}) %all-gather.5.cloned.1.call-update) | async-done | bytes 4194320 | tf_op jit(solution)/shard_map/all_gather | solution.py:124
  155.8 28.6 %all-gather.7.cloned.1.call-done = bf16[4,32,16,2048]{3,2,1,0:T(8,128)(2,1)} async-done(((bf16[2,32,16,2048]{3,2,1,0:T(8,128)(2,1)}), bf16[4,32,16,2048]{3,2,1,0:T(8,128)(2,1)}) %all-gather.7.cloned.1.call-update) | async-done | bytes 8388624 | tf_op jit(solution)/shard_map/all_gather | solution.py:125
  184.5 4.7 fusion.6
  189.2 3.6 multiply_convert_fusion
  192.8 4.5 convolution_convert_fusion.1
  197.3 4.3 convolution_convert_fusion
  201.6 8.3 %pad_maximum_fusion = bf16[2048,2048]{0,1:T(8,128)(2,1)} fusion(bf16[2048,1024]{0,1:T(8,128)(2,1)} %convolution_convert_fusion, bf16[2048,1024]{0,1:T(8,128)(2,1)} %convolution_convert_fusion.1), kind=kLoop, calls=%fused_computation.1 | loop fusion | flops 16777216 | bytes 16777216 | tf_op jit(solution)/shard_map/concatenate | solution.py:154
  210.0 12.3 %copy.48 = bf16[2048,2048]{1,0:T(8,128)(2,1)} copy(bf16[2048,2048]{0,1:T(8,128)(2,1)} %pad_maximum_fusion) | data formatting | bytes 16777216 | tf_op jit(solution)/shard_map/concatenate | solution.py:154
  222.3 23.1 %reduce-scatter.3.cloned.1.call-done = bf16[1,2,32,16,2048]{4,3,2,1,0:T(8,128)(2,1)} async-done(((bf16[2,2,32,16,2048]{4,3,2,1,0:T(8,128)(2,1)}), bf16[1,2,32,16,2048]{4,3,2,1,0:T(8,128)(2,1)}) %reduce-scatter.3.cloned.1.call-update) | async-done | bytes 4194320 | tf_op jit(solution)/shard_map/reduce_scatter | solution.py:155
  245.4 62.4 %reduce-scatter.5.cloned.1.call-done = bf16[1,1,32,16,2048]{4,3,2,1,0:T(8,128)(2,1)} async-done(((bf16[1,2,32,16,2048]{4,3,2,1,0:T(8,128)(2,1)}), bf16[1,1,32,16,2048]{4,3,2,1,0:T(8,128)(2,1)}) %reduce-scatter.5.cloned.1.call-update) | async-done | bytes 2097168 | tf_op jit(solution)/shard_map/reduce_scatter | solution.py:156
  307.8 9.6 %all-to-all-start.1 = ((bf16[32,16,2048]{2,1,0:T(8,128)(2,1)}), bf16[32,16,2048]{2,1,0:T(8,128)(2,1)S(1)}, u32[]{:S(2)}, u32[]{:S(2)}) async-start(bf16[32,16,2048]{2,1,0:T(8,128)(2,1)} %bitcast.181), calls=%async_computation.3 | async-start | bytes 4194304 | tf_op jit(solution)/shard_map/all_to_all | solution.py:158
  318.5 6.9 %fusion.11 = bf16[512,1024]{1,0:T(8,128)(2,1)} fusion(bf16[2048,2048]{1,0:T(8,128)(2,1)} %bitcast.281, f32[2048,512]{1,0:T(8,128)} %copy-done.48), kind=kOutput, calls=%fused_computation.47 | convolution fusion | flops 2153250816 | bytes 9437184 | tf_op jit(solution)/shard_map/dot_general | solution.py:138
  325.5 2.4 collective-permute-start.5
  327.8 38.0 %all-to-all-done.1 = bf16[32,16,2048]{2,1,0:T(8,128)(2,1)S(1)} async-done(((bf16[32,16,2048]{2,1,0:T(8,128)(2,1)}), bf16[32,16,2048]{2,1,0:T(8,128)(2,1)S(1)}, u32[]{:S(2)}, u32[]{:S(2)}) %all-to-all-start.1) | async-done | bytes 2097184 | tf_op jit(solution)/shard_map/all_to_all | solution.py:158
  365.8 2.3 gather_fusion
  368.2 1.8 gather.7
  370.1 1.3 fusion.24
  371.4 1.0 fusion.93
  373.1 0.8 fusion.89
  374.5 0.7 fusion.69
  375.7 3.3 concatenate.52
  379.1 5.2 fusion.8
  384.3 2.5 collective-permute-start.4
  386.8 21.3 %all-reduce.6.cloned.1.call-done = f32[64,1024]{1,0:T(8,128)} async-done(((f32[64,1024]{1,0:T(8,128)}), f32[64,1024]{1,0:T(8,128)}) %all-reduce.6.cloned.1.call-update) | async-done | bytes 262160 | tf_op jit(solution)/shard_map/psum | solution.py:183
  408.1 37.5 %all-reduce.8.cloned.1.call-done = f32[64,1024]{1,0:T(8,128)} async-done(((f32[64,1024]{1,0:T(8,128)}), f32[64,1024]{1,0:T(8,128)}) %all-reduce.8.cloned.1.call-update) | async-done | bytes 262160 | tf_op jit(solution)/shard_map/psum | solution.py:183
  445.8 3.3 add_bitcast_fusion
  449.1 3.5 collective-permute-start.2
  452.6 1.9 collective-permute-start.3
  454.6 39.8 %all-reduce.10.cloned.1.call-done = f32[64,1024]{1,0:T(8,128)} async-done(((f32[64,1024]{1,0:T(8,128)}), f32[64,1024]{1,0:T(8,128)}) %all-reduce.10.cloned.1.call-update) | async-done | bytes 262160 | tf_op jit(solution)/shard_map/psum | solution.py:183
  494.4 2.9 add_bitcast_fusion.1
  497.4 69.7 %all-reduce.12.cloned.1.call-done = f32[64,1024]{1,0:T(8,128)} async-done(((f32[64,1024]{1,0:T(8,128)}), f32[64,1024]{1,0:T(8,128)}) %all-reduce.12.cloned.1.call-update) | async-done | bytes 262160 | tf_op jit(solution)/shard_map/psum | solution.py:183
  567.3 2.8 fusion.158
  570.1 39.2 %all-reduce.14.cloned.1.call-done = f32[64,1024]{1,0:T(8,128)} async-done(((f32[64,1024]{1,0:T(8,128)}), f32[64,1024]{1,0:T(8,128)}) %all-reduce.14.cloned.1.call-update) | async-done | bytes 262160 | tf_op jit(solution)/shard_map/psum | solution.py:183
  609.3 1.4 slice.634
  610.7 1.6 slice_bitcast_fusion.2
  612.2 1.6 slice.633
  (157 shorter events, 7.0 us)
Async XLA Ops:
  7.2 182.0 %copy-start = (bf16[1,512,1024]{2,1,0:T(8,128)(2,1)S(1)}, bf16[1,512,1024]{2,1,0:T(8,128)(2,1)}, u32[]{:S(2)}) copy-start(bf16[1,512,1024]{2,1,0:T(8,128)(2,1)} %param.14) | copy-start | bytes 3145732
  7.2 25.0 %copy-start.5 = (bf16[1,128,1024]{2,1,0:T(8,128)(2,1)S(1)}, bf16[1,128,1024]{2,1,0:T(8,128)(2,1)}, u32[]{:S(2)}) copy-start(bf16[1,128,1024]{2,1,0:T(8,128)(2,1)} %param.15) | copy-start | bytes 786436
  7.2 148.4 %all-gather.5.cloned.1.call-start = ((), (), s32[]{:S(2)}) async-start(), calls=%async_computation.11 | async-start | bytes 6291456 | tf_op jit(solution)/shard_map/all_gather | solution.py:124
  8.1 11.6 %collective-permute-start = (bf16[15,1024]{1,0:T(8,128)(2,1)S(1)}, bf16[15,1024]{1,0:T(8,128)(2,1)S(1)}, u32[]{:S(2)}, u32[]{:S(2)}) collective-permute-start(bf16[15,1024]{1,0:T(8,128)(2,1)S(1)} %get-tuple-element.53), channel_id=1, source_target_pairs={{0,2},{2,4},{4,6},{6,8},{8,10},{10,12},{12,14},{14,16},{16,18},{18... | collective-permute-start | bytes 92168 | tf_op jit(solution)/shard_map/ppermute | solution.py:18
  12.6 7.1 %collective-permute-start.1 = (bf16[15,1024]{1,0:T(8,128)(2,1)S(1)}, bf16[15,1024]{1,0:T(8,128)(2,1)S(1)}, u32[]{:S(2)}, u32[]{:S(2)}) collective-permute-start(bf16[15,1024]{1,0:T(8,128)(2,1)S(1)} %get-tuple-element.54), channel_id=1, source_target_pairs={{2,0},{4,2},{6,4},{8,6},{10,8},{12,10},{14,12},{16,14},{18,16},{20... | collective-permute-start | bytes 92168 | tf_op jit(solution)/shard_map/ppermute | solution.py:19
  17.9 11.1 %copy-start.9 = (f32[1,1024]{1,0:T(1,128)}, f32[1,1024]{1,0:T(1,128)S(1)}, u32[]{:S(2)}) copy-start(f32[1,1024]{1,0:T(1,128)S(1)} %get-tuple-element.63) | copy-start | bytes 12292
  17.9 11.1 %copy-start.11 = (f32[1,1024]{1,0:T(1,128)}, f32[1,1024]{1,0:T(1,128)S(1)}, u32[]{:S(2)}) copy-start(f32[1,1024]{1,0:T(1,128)S(1)} %get-tuple-element.64) | copy-start | bytes 12292
  17.9 11.1 %copy-start.13 = (f32[1,1024]{1,0:T(1,128)}, f32[1,1024]{1,0:T(1,128)S(1)}, u32[]{:S(2)}) copy-start(f32[1,1024]{1,0:T(1,128)S(1)} %get-tuple-element.65) | copy-start | bytes 12292
  17.9 11.1 %copy-start.15 = (f32[1,1024]{1,0:T(1,128)}, f32[1,1024]{1,0:T(1,128)S(1)}, u32[]{:S(2)}) copy-start(f32[1,1024]{1,0:T(1,128)S(1)} %get-tuple-element.66) | copy-start | bytes 12292
  17.9 11.1 %copy-start.17 = (f32[1,1024]{1,0:T(1,128)}, f32[1,1024]{1,0:T(1,128)S(1)}, u32[]{:S(2)}) copy-start(f32[1,1024]{1,0:T(1,128)S(1)} %get-tuple-element.67) | copy-start | bytes 12292
  17.9 11.1 %copy-start.19 = (f32[1,1024]{1,0:T(1,128)}, f32[1,1024]{1,0:T(1,128)S(1)}, u32[]{:S(2)}) copy-start(f32[1,1024]{1,0:T(1,128)S(1)} %get-tuple-element.68) | copy-start | bytes 12292
  17.9 11.1 %copy-start.21 = (f32[1,1024]{1,0:T(1,128)}, f32[1,1024]{1,0:T(1,128)S(1)}, u32[]{:S(2)}) copy-start(f32[1,1024]{1,0:T(1,128)S(1)} %get-tuple-element.69) | copy-start | bytes 12292
  17.9 11.1 %copy-start.23 = (f32[1,1024]{1,0:T(1,128)}, f32[1,1024]{1,0:T(1,128)S(1)}, u32[]{:S(2)}) copy-start(f32[1,1024]{1,0:T(1,128)S(1)} %get-tuple-element.70) | copy-start | bytes 12292
  18.0 11.1 %copy-start.25 = (f32[1,1024]{1,0:T(1,128)}, f32[1,1024]{1,0:T(1,128)S(1)}, u32[]{:S(2)}) copy-start(f32[1,1024]{1,0:T(1,128)S(1)} %get-tuple-element.71) | copy-start | bytes 12292
  18.0 11.1 %copy-start.27 = (f32[1,1024]{1,0:T(1,128)}, f32[1,1024]{1,0:T(1,128)S(1)}, u32[]{:S(2)}) copy-start(f32[1,1024]{1,0:T(1,128)S(1)} %get-tuple-element.72) | copy-start | bytes 12292
  18.0 11.1 %copy-start.29 = (f32[1,1024]{1,0:T(1,128)}, f32[1,1024]{1,0:T(1,128)S(1)}, u32[]{:S(2)}) copy-start(f32[1,1024]{1,0:T(1,128)S(1)} %get-tuple-element.73) | copy-start | bytes 12292
  18.9 10.2 %copy-start.31 = (s32[256]{0:T(256)}, s32[256]{0:T(256)S(1)}, u32[]{:S(2)}) copy-start(s32[256]{0:T(256)S(1)} %fusion.161) | copy-start | bytes 3076
  19.7 14.2 %copy-start.34 = (s32[128]{0:T(128)}, s32[128]{0:T(128)S(1)}, u32[]{:S(2)}) copy-start(s32[128]{0:T(128)S(1)} %get-tuple-element.86) | copy-start | bytes 1540
  19.7 14.2 %copy-start.36 = (s32[128]{0:T(128)}, s32[128]{0:T(128)S(1)}, u32[]{:S(2)}) copy-start(s32[128]{0:T(128)S(1)} %get-tuple-element.87) | copy-start | bytes 1540
  91.9 92.6 %copy-start.47 = (bf16[1,1024,512]{2,1,0:T(8,128)(2,1)S(1)}, bf16[1,1024,512]{2,1,0:T(8,128)(2,1)}, u32[]{:S(2)}) copy-start(bf16[1,1024,512]{2,1,0:T(8,128)(2,1)} %param.13) | copy-start | bytes 3145732
  91.9 92.5 %all-gather.7.cloned.1.call-start = ((), (), s32[]{:S(2)}) async-start(), calls=%async_computation.12 | async-start | bytes 12582912 | tf_op jit(solution)/shard_map/all_gather | solution.py:125
  155.6 89.8 %reduce-scatter.3.cloned.1.call-start = ((), (), s32[]{:S(2)}) async-start(), calls=%async_computation.4 | async-start | bytes 12582912 | tf_op jit(solution)/shard_map/reduce_scatter | solution.py:155
  222.3 85.5 %reduce-scatter.5.cloned.1.call-start = ((), (), s32[]{:S(2)}) async-start(), calls=%async_computation.5 | async-start | bytes 6291456 | tf_op jit(solution)/shard_map/reduce_scatter | solution.py:156
  245.4 72.1 %copy-start.32 = (s32[256]{0:T(256)S(1)}, s32[256]{0:T(256)}, u32[]{:S(2)}) copy-start(s32[256]{0:T(256)} %copy-done.31) | copy-start | bytes 3076
  245.4 72.2 %copy-start.33 = (s32[1,128,2]{1,2,0:T(2,128)S(1)}, s32[1,128,2]{1,2,0:T(2,128)}, u32[]{:S(2)}) copy-start(s32[1,128,2]{1,2,0:T(2,128)} %param.12) | copy-start | bytes 3076
  307.8 58.0 %all-to-all-start.1 = ((bf16[32,16,2048]{2,1,0:T(8,128)(2,1)}), bf16[32,16,2048]{2,1,0:T(8,128)(2,1)S(1)}, u32[]{:S(2)}, u32[]{:S(2)}) async-start(bf16[32,16,2048]{2,1,0:T(8,128)(2,1)} %bitcast.181), calls=%async_computation.3 | async-start | bytes 4194304 | tf_op jit(solution)/shard_map/all_to_all | solution.py:158
  317.4 90.6 %all-reduce.6.cloned.1.call-start = ((), (), s32[]{:S(2)}) async-start(), calls=%async_computation.6 | async-start | bytes 524288 | tf_op jit(solution)/shard_map/psum | solution.py:183
  325.5 120.4 %collective-permute-start.5 = (bf16[512,1024]{1,0:T(8,128)(2,1)}, bf16[512,1024]{1,0:T(8,128)(2,1)}, u32[]{:S(2)}, u32[]{:S(2)}) collective-permute-start(bf16[512,1024]{1,0:T(8,128)(2,1)} %fusion.11), channel_id=1, source_target_pairs={{0,1},{1,0},{2,3},{3,2},{4,5},{5,4},{6,7},{7,6},{8,9},{9,8},{10,11... | collective-permute-start | bytes 3145736 | tf_op jit(solution)/shard_map/ppermute | solution.py:146
  368.2 4.9 copy-start.4
  379.0 66.6 %all-reduce.8.cloned.1.call-start = ((), (), s32[]{:S(2)}) async-start(), calls=%async_computation.7 | async-start | bytes 524288 | tf_op jit(solution)/shard_map/psum | solution.py:183
  384.3 110.1 %collective-permute-start.4 = (bf16[1024,512]{1,0:T(8,128)(2,1)S(1)}, bf16[1024,512]{1,0:T(8,128)(2,1)}, u32[]{:S(2)}, u32[]{:S(2)}) collective-permute-start(bf16[1024,512]{1,0:T(8,128)(2,1)S(1)} %fusion.8), channel_id=1, source_target_pairs={{0,1},{1,0},{2,3},{3,2},{4,5},{5,4},{6,7},{7,6},{8,9},{9,8},{10,11... | collective-permute-start | bytes 3145736 | tf_op jit(solution)/shard_map/ppermute | solution.py:145
  408.1 86.3 %all-reduce.10.cloned.1.call-start = ((), (), s32[]{:S(2)}) async-start(), calls=%async_computation.8 | async-start | bytes 524288 | tf_op jit(solution)/shard_map/psum | solution.py:183
  445.7 121.6 %copy-start.10 = (f32[1,1024]{1,0:T(1,128)S(1)}, f32[1,1024]{1,0:T(1,128)}, u32[]{:S(2)}) copy-start(f32[1,1024]{1,0:T(1,128)} %copy-done.9) | copy-start | bytes 12292
  445.7 121.6 %copy-start.12 = (f32[1,1024]{1,0:T(1,128)S(1)}, f32[1,1024]{1,0:T(1,128)}, u32[]{:S(2)}) copy-start(f32[1,1024]{1,0:T(1,128)} %copy-done.11) | copy-start | bytes 12292
  445.7 121.5 %copy-start.14 = (f32[1,1024]{1,0:T(1,128)S(1)}, f32[1,1024]{1,0:T(1,128)}, u32[]{:S(2)}) copy-start(f32[1,1024]{1,0:T(1,128)} %copy-done.13) | copy-start | bytes 12292
  445.7 121.5 %copy-start.16 = (f32[1,1024]{1,0:T(1,128)S(1)}, f32[1,1024]{1,0:T(1,128)}, u32[]{:S(2)}) copy-start(f32[1,1024]{1,0:T(1,128)} %copy-done.15) | copy-start | bytes 12292
  445.7 121.5 %copy-start.18 = (f32[1,1024]{1,0:T(1,128)S(1)}, f32[1,1024]{1,0:T(1,128)}, u32[]{:S(2)}) copy-start(f32[1,1024]{1,0:T(1,128)} %copy-done.17) | copy-start | bytes 12292
  445.7 121.5 %copy-start.20 = (f32[1,1024]{1,0:T(1,128)S(1)}, f32[1,1024]{1,0:T(1,128)}, u32[]{:S(2)}) copy-start(f32[1,1024]{1,0:T(1,128)} %copy-done.19) | copy-start | bytes 12292
  445.7 121.5 %copy-start.22 = (f32[1,1024]{1,0:T(1,128)S(1)}, f32[1,1024]{1,0:T(1,128)}, u32[]{:S(2)}) copy-start(f32[1,1024]{1,0:T(1,128)} %copy-done.21) | copy-start | bytes 12292
  445.7 121.5 %copy-start.24 = (f32[1,1024]{1,0:T(1,128)S(1)}, f32[1,1024]{1,0:T(1,128)}, u32[]{:S(2)}) copy-start(f32[1,1024]{1,0:T(1,128)} %copy-done.23) | copy-start | bytes 12292
  445.7 121.5 %copy-start.26 = (f32[1,1024]{1,0:T(1,128)S(1)}, f32[1,1024]{1,0:T(1,128)}, u32[]{:S(2)}) copy-start(f32[1,1024]{1,0:T(1,128)} %copy-done.25) | copy-start | bytes 12292
  445.7 121.5 %copy-start.28 = (f32[1,1024]{1,0:T(1,128)S(1)}, f32[1,1024]{1,0:T(1,128)}, u32[]{:S(2)}) copy-start(f32[1,1024]{1,0:T(1,128)} %copy-done.27) | copy-start | bytes 12292
  445.8 121.5 %copy-start.30 = (f32[1,1024]{1,0:T(1,128)S(1)}, f32[1,1024]{1,0:T(1,128)}, u32[]{:S(2)}) copy-start(f32[1,1024]{1,0:T(1,128)} %copy-done.29) | copy-start | bytes 12292
  445.8 121.4 %all-reduce.12.cloned.1.call-start = ((), (), s32[]{:S(2)}) async-start(), calls=%async_computation.9 | async-start | bytes 524288 | tf_op jit(solution)/shard_map/psum | solution.py:183
  449.1 48.2 %collective-permute-start.2 = (bf16[15,1024]{1,0:T(8,128)(2,1)S(1)}, bf16[15,1024]{1,0:T(8,128)(2,1)S(1)}, u32[]{:S(2)}, u32[]{:S(2)}) collective-permute-start(bf16[15,1024]{1,0:T(8,128)(2,1)S(1)} %get-tuple-element.49), channel_id=1, source_target_pairs={{0,2},{2,4},{4,6},{6,8},{8,10},{10,12},{12,14},{14,16},{16,18},{18... | collective-permute-start | bytes 92168 | tf_op jit(solution)/shard_map/ppermute | solution.py:18
  452.6 44.7 %collective-permute-start.3 = (bf16[15,1024]{1,0:T(8,128)(2,1)S(1)}, bf16[15,1024]{1,0:T(8,128)(2,1)S(1)}, u32[]{:S(2)}, u32[]{:S(2)}) collective-permute-start(bf16[15,1024]{1,0:T(8,128)(2,1)S(1)} %get-tuple-element.50), channel_id=1, source_target_pairs={{2,0},{4,2},{6,4},{8,6},{10,8},{12,10},{14,12},{16,14},{18,16},{20... | collective-permute-start | bytes 92168 | tf_op jit(solution)/shard_map/ppermute | solution.py:19
  494.4 114.9 %all-reduce.14.cloned.1.call-start = ((), (), s32[]{:S(2)}) async-start(), calls=%async_computation.10 | async-start | bytes 524288 | tf_op jit(solution)/shard_map/psum | solution.py:183
  567.3 46.5 %copy-start.1 = (bf16[1,512,1024]{2,1,0:T(8,128)(2,1)S(1)}, bf16[1,512,1024]{2,1,0:T(8,128)(2,1)}, u32[]{:S(2)}) copy-start(bf16[1,512,1024]{2,1,0:T(8,128)(2,1)} %param.14) | copy-start | bytes 3145732
  (18 other events, 59.2 us)
Sparse Core Ops, SparseCore 0:
  92.1 63.4 all-gather.4
  157.4 27.0 all-gather.6
  222.4 22.9 reduce-scatter.2
  247.8 59.9 reduce-scatter.4
  379.2 28.8 all-reduce.5
  410.5 35.0 all-reduce.7
  447.9 46.3 all-reduce.9
  496.7 70.4 all-reduce.11
  569.8 39.5 all-reduce.13
where the time goes:
time: 621 us; the launch traced here: 620 us
  waiting for transfers between devices  423 us (68%)
  blocking collectives  58 us (9%)
  other arithmetic  36 us (6%)
  matrix products  31.6 us (5%)
  local copies, waits for them, and re-layouts  29.8 us (5%)
  starting transfers between devices  26.8 us (4%)
  between operations  14.8 us (2%)
    psum x5, waiting for transfers between devices, body(): small = lax.psum(small, axis)  208 us
    all_gather x1, waiting for transfers between devices, body(): arrived = lax.all_gather(arrived, 'xl', axis=0, tiled=False)  63.6 us
    reduce_scatter x1, waiting for transfers between devices, body(): back = lax.psum_scatter(back, 'xl', scatter_dimension=1, tiled=True)  62.4 us
    all_to_all x1, blocking collectives, body(): lax.all_to_all(packed, GRP, split_axis=0, concat_axis=0, tiled=True)  58 us
    all_to_all x1, waiting for transfers between devices, body(): totals = lax.all_to_all(back, GRP, split_axis=0, concat_axis=0, tiled=True)  38 us
    all_gather x1, waiting for transfers between devices, body(): arrived = lax.all_gather(arrived, 'c', axis=0, tiled=False)  28.6 us
    reduce_scatter x1, waiting for transfers between devices, body(): back = lax.psum_scatter(back, 'c', scatter_dimension=0, tiled=True)  23.1 us
  transfers between devices with their start and end apart: 16, of which 10 were waited for; matrix products, arithmetic and copies ran while one was open for 6% of the time, Pallas kernels for 0%

commit v1 on v0

--- a/solution.py
+++ b/solution.py
@@ -3,6 +3,7 @@
 from jax import lax
 from jax.sharding import Mesh
 from jax.sharding import PartitionSpec as P
+from jax.lax import all_gather
 
 eps = 1e-06
 SEQ = ("z", "y", "xl", "c")
@@ -180,7 +181,10 @@
     kernel_term = kernel_terms(padded, upstream_total, length, row_count)
     small = jnp.concatenate([kernel_term, gain_term[None, :], router_term.T], axis=0)
     for axis in ("c", "xl", "y", "z", "dp"):
-        small = lax.psum(small, axis)
+        name_racks = lambda piece_in, shard_axis: jnp.sum(
+            all_gather(piece_in, axis_name=shard_axis), axis=0
+        )
+        small = name_racks(small, axis)
     grad_kernel = small[:length]
     grad_gain = small[length]
     grad_router = small[length + 1 :].T

time: 621 us -> 498 us (0.80)
  waiting for transfers between devices: 423 us -> 272 us
  blocking collectives: 58 us -> 78.1 us
  other arithmetic: 36 us -> 42.6 us
    psum x5 -> x0, waiting for transfers between devices: 208 us -> none  [body(): small = lax.psum(small, axis)]
    all_gather x0 -> x2, waiting for transfers between devices: none -> 22.3 us  [body(): all_gather(piece_in, axis_name=shard_axis)]
    all_gather x0 -> x3, blocking collectives: none -> 20.1 us  [body(): all_gather(piece_in, axis_name=shard_axis)]
    ppermute x1, waiting for transfers between devices: 0.01 us -> 16.1 us  [body(): out_other = lax.ppermute(out_mine, 'dp', dp_pair)]
    all_to_all x1, waiting for transfers between devices: 38 us -> 47.1 us  [body(): totals = lax.all_to_all(back, GRP, split_axis=0, concat_axis=0, tiled=True)]
    ppermute x1, waiting for transfers between devices: 0.01 us -> 7.45 us  [body(): in_other = lax.ppermute(in_mine, 'dp', dp_pair)]
    ppermute x2, starting transfers between devices: 8.02 us -> 14.3 us  [padded_2(): before = lax.ppermute(last, axis, up)]
  transfers between devices with their start and end apart: 16 -> 13, of which waited for: 10 -> 9; matrix products, arithmetic and copies ran while one was open for 6% -> 5% of each run, Pallas kernels for 0% -> 0%
where the time goes in v1:
time: 498 us; the launch traced here: 494 us
  waiting for transfers between devices  272 us (55%)
  blocking collectives  78.1 us (16%)
  other arithmetic  42.6 us (9%)
  starting transfers between devices  31.4 us (6%)
  matrix products  30.9 us (6%)
  local copies, waits for them, and re-layouts  24.1 us (5%)
  between operations  15.1 us (3%)
    all_gather x1, waiting for transfers between devices, body(): arrived = lax.all_gather(arrived, 'xl', axis=0, tiled=False)  63.6 us
    reduce_scatter x1, waiting for transfers between devices, body(): back = lax.psum_scatter(back, 'xl', scatter_dimension=1, tiled=True)  62.4 us
    all_to_all x1, blocking collectives, body(): lax.all_to_all(packed, GRP, split_axis=0, concat_axis=0, tiled=True)  58 us
    all_to_all x1, waiting for transfers between devices, body(): totals = lax.all_to_all(back, GRP, split_axis=0, concat_axis=0, tiled=True)  47.1 us
    all_gather x1, waiting for transfers between devices, body(): arrived = lax.all_gather(arrived, 'c', axis=0, tiled=False)  28.6 us
    reduce_scatter x1, waiting for transfers between devices, body(): back = lax.psum_scatter(back, 'c', scatter_dimension=0, tiled=True)  23.1 us
    all_gather x2, waiting for transfers between devices, body(): all_gather(piece_in, axis_name=shard_axis)  22.3 us
    all_gather x3, blocking collectives, body(): all_gather(piece_in, axis_name=shard_axis)  20.1 us
  transfers between devices with their start and end apart: 13, of which 9 were waited for; matrix products, arithmetic and copies ran while one was open for 5% of the time, Pallas kernels for 0%

profile of v1, /device:TPU:1, one launch (start us, length us, event | category | flops | bytes accessed | tf_op | source)
XLA Modules:
  0.0 494.0 jit_solution(8661614581285304783)
XLA Ops:
  7.2 0.9 slice_bitcast_fusion.4
  8.1 4.5 collective-permute-start
  12.6 1.9 collective-permute-start.1
  14.6 0.8 copy.52
  15.6 1.0 slice_convert_fusion.29
  16.7 1.2 slice_convert_fusion.30
  18.9 0.8 slice_bitcast_fusion.6
  19.7 11.3 %multiply_reduce_fusion.2 = (f32[128]{0:T(128)S(1)}, f32[128,1024]{1,0:T(8,128)S(1)}) fusion(bf16[15,1024]{1,0:T(8,128)(2,1)S(1)} %collective-permute-done.1, bf16[128,1024]{1,0:T(8,128)(2,1)} %bitcast.180, f32[1024]{0:T(1024)S(1)} %bitcast.212, f32[1024]{0:T(1024)S(1)} %bitcast.214, f32[1024]{0:T(1024)S(1)} %bitcast.218, f32[1024]{0:T(1024)S(1)} %bitcast.220, ...), kind=kLoop, calls=%fused_computation.269 | loop fusion | flops 24248192 | bytes 975360 | tf_op jit(solution)/shard_map/reduce_sum | solution.py:52
  31.8 0.8 multiply_convert_fusion.2
  32.6 1.0 fusion.16
  35.2 0.7 convolution_convert_fusion.2
  36.0 58.0 %all_to_all.10 = bf16[32,16,2048]{2,1,0:T(8,128)(2,1)} all-to-all(bf16[32,16,2048]{2,1,0:T(8,128)(2,1)S(1)} %bitcast.179), channel_id=1, replica_groups=mesh['z'=8,'y'=4,'xl'=2,'c'=2,'dp'=2] {'z','y'}, dimensions={0} | all-to-all | bytes 4194304 | tf_op jit(solution)/shard_map/all_to_all | solution.py:124
  94.0 63.6 %all-gather.12.cloned.1.call-done = bf16[64,16,2048]{2,1,0:T(8,128)(2,1)} async-done(((bf16[32,16,2048]{2,1,0:T(8,128)(2,1)}), bf16[64,16,2048]{2,1,0:T(8,128)(2,1)}) %all-gather.12.cloned.1.call-update) | async-done | bytes 4194320 | tf_op jit(solution)/shard_map/all_gather | solution.py:125
  157.9 28.6 %all-gather.14.cloned.1.call-done = bf16[4,32,16,2048]{3,2,1,0:T(8,128)(2,1)} async-done(((bf16[2,32,16,2048]{3,2,1,0:T(8,128)(2,1)}), bf16[4,32,16,2048]{3,2,1,0:T(8,128)(2,1)}) %all-gather.14.cloned.1.call-update) | async-done | bytes 8388624 | tf_op jit(solution)/shard_map/all_gather | solution.py:126
  186.5 4.7 fusion.6
  191.3 3.5 multiply_convert_fusion
  194.8 4.5 convolution_convert_fusion.1
  199.3 4.3 convolution_convert_fusion
  203.7 8.3 %pad_maximum_fusion = bf16[2048,2048]{0,1:T(8,128)(2,1)} fusion(bf16[2048,1024]{0,1:T(8,128)(2,1)} %convolution_convert_fusion, bf16[2048,1024]{0,1:T(8,128)(2,1)} %convolution_convert_fusion.1), kind=kLoop, calls=%fused_computation.1 | loop fusion | flops 16777216 | bytes 16777216 | tf_op jit(solution)/shard_map/concatenate | solution.py:155
  212.0 12.3 %copy.57 = bf16[2048,2048]{1,0:T(8,128)(2,1)} copy(bf16[2048,2048]{0,1:T(8,128)(2,1)} %pad_maximum_fusion) | data formatting | bytes 16777216 | tf_op jit(solution)/shard_map/concatenate | solution.py:155
  224.4 23.1 %reduce-scatter.3.cloned.1.call-done = bf16[1,2,32,16,2048]{4,3,2,1,0:T(8,128)(2,1)} async-done(((bf16[2,2,32,16,2048]{4,3,2,1,0:T(8,128)(2,1)}), bf16[1,2,32,16,2048]{4,3,2,1,0:T(8,128)(2,1)}) %reduce-scatter.3.cloned.1.call-update) | async-done | bytes 4194320 | tf_op jit(solution)/shard_map/reduce_scatter | solution.py:156
  247.5 62.4 %reduce-scatter.5.cloned.1.call-done = bf16[1,1,32,16,2048]{4,3,2,1,0:T(8,128)(2,1)} async-done(((bf16[1,2,32,16,2048]{4,3,2,1,0:T(8,128)(2,1)}), bf16[1,1,32,16,2048]{4,3,2,1,0:T(8,128)(2,1)}) %reduce-scatter.5.cloned.1.call-update) | async-done | bytes 2097168 | tf_op jit(solution)/shard_map/reduce_scatter | solution.py:157
  309.9 9.6 %all-to-all-start.1 = ((bf16[32,16,2048]{2,1,0:T(8,128)(2,1)}), bf16[32,16,2048]{2,1,0:T(8,128)(2,1)S(1)}, u32[]{:S(2)}, u32[]{:S(2)}) async-start(bf16[32,16,2048]{2,1,0:T(8,128)(2,1)} %bitcast.187), calls=%async_computation.3 | async-start | bytes 4194304 | tf_op jit(solution)/shard_map/all_to_all | solution.py:159
  320.8 47.1 %all-to-all-done.1 = bf16[32,16,2048]{2,1,0:T(8,128)(2,1)S(1)} async-done(((bf16[32,16,2048]{2,1,0:T(8,128)(2,1)}), bf16[32,16,2048]{2,1,0:T(8,128)(2,1)S(1)}, u32[]{:S(2)}, u32[]{:S(2)}) %all-to-all-start.1) | async-done | bytes 2097184 | tf_op jit(solution)/shard_map/all_to_all | solution.py:159
  367.9 2.3 gather_fusion
  370.3 1.8 gather.7
  372.1 1.3 fusion.24
  373.5 1.0 fusion.93
  375.2 0.8 fusion.89
  378.0 4.5 all-gather.2
  382.6 8.2 %all-gather.3 = f32[128,1024]{1,0:T(8,128)S(1)} all-gather(f32[64,1024]{1,0:T(8,128)S(1)} %reduce_sum.443), channel_id=5, replica_groups=mesh['z'=8,'y'=4,'xl'=2,'c'=2,'dp'=2] {'xl'}, dimensions={0}, use_global_device_ids=true | all-gather | bytes 786432 | tf_op jit(solution)/shard_map/all_gather | solution.py:185
  390.7 0.7 reduce_sum.444
  391.5 22.3 %all-gather.16.cloned.1.call-done = f32[256,1024]{1,0:T(8,128)} async-done(((f32[64,1024]{1,0:T(8,128)}), f32[256,1024]{1,0:T(8,128)}) %all-gather.16.cloned.1.call-update) | async-done | bytes 1048592 | tf_op jit(solution)/shard_map/all_gather | solution.py:185
  413.9 2.0 reduce_sum.445
  415.9 7.0 %fusion.11 = bf16[512,1024]{1,0:T(8,128)(2,1)} fusion(bf16[2048,2048]{1,0:T(8,128)(2,1)} %bitcast.291, f32[2048,512]{1,0:T(8,128)} %copy-done.48), kind=kOutput, calls=%fused_computation.47 | convolution fusion | flops 2153250816 | bytes 9437184 | tf_op jit(solution)/shard_map/dot_general | solution.py:139
  422.9 2.7 collective-permute-start.5
  425.6 4.5 fusion.8
  430.6 16.1 %collective-permute-done.5 = bf16[512,1024]{1,0:T(8,128)(2,1)} collective-permute-done((bf16[512,1024]{1,0:T(8,128)(2,1)}, bf16[512,1024]{1,0:T(8,128)(2,1)}, u32[]{:S(2)}, u32[]{:S(2)}) %collective-permute-start.5) | collective-permute-done | bytes 1048608 | tf_op jit(solution)/shard_map/ppermute | solution.py:147
  446.7 3.3 add_bitcast_fusion
  450.0 9.8 %collective-permute-start.2 = (bf16[15,1024]{1,0:T(8,128)(2,1)S(1)}, bf16[15,1024]{1,0:T(8,128)(2,1)S(1)}, u32[]{:S(2)}, u32[]{:S(2)}) collective-permute-start(bf16[15,1024]{1,0:T(8,128)(2,1)S(1)} %get-tuple-element.49), channel_id=1, source_target_pairs={{0,2},{2,4},{4,6},{6,8},{8,10},{10,12},{12,14},{14,16},{16,18},{18... | collective-permute-start | bytes 92168 | tf_op jit(solution)/shard_map/ppermute | solution.py:19
  459.8 1.9 collective-permute-start.3
  461.7 7.4 %collective-permute-done.4 = bf16[1024,512]{1,0:T(8,128)(2,1)} collective-permute-done((bf16[1024,512]{1,0:T(8,128)(2,1)S(1)}, bf16[1024,512]{1,0:T(8,128)(2,1)}, u32[]{:S(2)}, u32[]{:S(2)}) %collective-permute-start.4) | collective-permute-done | bytes 1048608 | tf_op jit(solution)/shard_map/ppermute | solution.py:146
  469.1 2.9 add_bitcast_fusion.1
  472.0 1.0 collective-permute-done.3
  473.3 2.8 fusion.158
  476.0 1.7 reduce_sum.446
  477.8 7.4 %all-gather.6 = f32[128,1024]{1,0:T(8,128)S(1)} all-gather(f32[64,1024]{1,0:T(8,128)S(1)} %reduce_sum.446), channel_id=8, replica_groups=mesh['z'=8,'y'=4,'xl'=2,'c'=2,'dp'=2] {'dp'}, dimensions={0}, use_global_device_ids=true | all-gather | bytes 786432 | tf_op jit(solution)/shard_map/all_gather | solution.py:185
  485.8 0.7 slice_bitcast_fusion.2
  (158 shorter events, 9.6 us)
Async XLA Ops:
  7.2 184.1 %copy-start = (bf16[1,512,1024]{2,1,0:T(8,128)(2,1)S(1)}, bf16[1,512,1024]{2,1,0:T(8,128)(2,1)}, u32[]{:S(2)}) copy-start(bf16[1,512,1024]{2,1,0:T(8,128)(2,1)} %param.14) | copy-start | bytes 3145732
  7.2 27.0 %copy-start.5 = (bf16[1,128,1024]{2,1,0:T(8,128)(2,1)S(1)}, bf16[1,128,1024]{2,1,0:T(8,128)(2,1)}, u32[]{:S(2)}) copy-start(bf16[1,128,1024]{2,1,0:T(8,128)(2,1)} %param.15) | copy-start | bytes 786436
  7.2 150.4 %all-gather.12.cloned.1.call-start = ((), (), s32[]{:S(2)}) async-start(), calls=%async_computation.6 | async-start | bytes 6291456 | tf_op jit(solution)/shard_map/all_gather | solution.py:125
  8.1 11.6 %collective-permute-start = (bf16[15,1024]{1,0:T(8,128)(2,1)S(1)}, bf16[15,1024]{1,0:T(8,128)(2,1)S(1)}, u32[]{:S(2)}, u32[]{:S(2)}) collective-permute-start(bf16[15,1024]{1,0:T(8,128)(2,1)S(1)} %get-tuple-element.53), channel_id=1, source_target_pairs={{0,2},{2,4},{4,6},{6,8},{8,10},{10,12},{12,14},{14,16},{16,18},{18... | collective-permute-start | bytes 92168 | tf_op jit(solution)/shard_map/ppermute | solution.py:19
  12.6 7.1 %collective-permute-start.1 = (bf16[15,1024]{1,0:T(8,128)(2,1)S(1)}, bf16[15,1024]{1,0:T(8,128)(2,1)S(1)}, u32[]{:S(2)}, u32[]{:S(2)}) collective-permute-start(bf16[15,1024]{1,0:T(8,128)(2,1)S(1)} %get-tuple-element.54), channel_id=1, source_target_pairs={{2,0},{4,2},{6,4},{8,6},{10,8},{12,10},{14,12},{16,14},{18,16},{20... | collective-permute-start | bytes 92168 | tf_op jit(solution)/shard_map/ppermute | solution.py:20
  17.9 13.2 %copy-start.9 = (f32[1,1024]{1,0:T(1,128)}, f32[1,1024]{1,0:T(1,128)S(1)}, u32[]{:S(2)}) copy-start(f32[1,1024]{1,0:T(1,128)S(1)} %get-tuple-element.63) | copy-start | bytes 12292
  17.9 13.2 %copy-start.11 = (f32[1,1024]{1,0:T(1,128)}, f32[1,1024]{1,0:T(1,128)S(1)}, u32[]{:S(2)}) copy-start(f32[1,1024]{1,0:T(1,128)S(1)} %get-tuple-element.64) | copy-start | bytes 12292
  17.9 13.2 %copy-start.13 = (f32[1,1024]{1,0:T(1,128)}, f32[1,1024]{1,0:T(1,128)S(1)}, u32[]{:S(2)}) copy-start(f32[1,1024]{1,0:T(1,128)S(1)} %get-tuple-element.65) | copy-start | bytes 12292
  17.9 13.2 %copy-start.15 = (f32[1,1024]{1,0:T(1,128)}, f32[1,1024]{1,0:T(1,128)S(1)}, u32[]{:S(2)}) copy-start(f32[1,1024]{1,0:T(1,128)S(1)} %get-tuple-element.66) | copy-start | bytes 12292
  17.9 13.2 %copy-start.17 = (f32[1,1024]{1,0:T(1,128)}, f32[1,1024]{1,0:T(1,128)S(1)}, u32[]{:S(2)}) copy-start(f32[1,1024]{1,0:T(1,128)S(1)} %get-tuple-element.67) | copy-start | bytes 12292
  17.9 13.2 %copy-start.19 = (f32[1,1024]{1,0:T(1,128)}, f32[1,1024]{1,0:T(1,128)S(1)}, u32[]{:S(2)}) copy-start(f32[1,1024]{1,0:T(1,128)S(1)} %get-tuple-element.68) | copy-start | bytes 12292
  17.9 13.2 %copy-start.21 = (f32[1,1024]{1,0:T(1,128)}, f32[1,1024]{1,0:T(1,128)S(1)}, u32[]{:S(2)}) copy-start(f32[1,1024]{1,0:T(1,128)S(1)} %get-tuple-element.69) | copy-start | bytes 12292
  17.9 13.2 %copy-start.23 = (f32[1,1024]{1,0:T(1,128)}, f32[1,1024]{1,0:T(1,128)S(1)}, u32[]{:S(2)}) copy-start(f32[1,1024]{1,0:T(1,128)S(1)} %get-tuple-element.70) | copy-start | bytes 12292
  17.9 13.2 %copy-start.25 = (f32[1,1024]{1,0:T(1,128)}, f32[1,1024]{1,0:T(1,128)S(1)}, u32[]{:S(2)}) copy-start(f32[1,1024]{1,0:T(1,128)S(1)} %get-tuple-element.71) | copy-start | bytes 12292
  17.9 13.2 %copy-start.27 = (f32[1,1024]{1,0:T(1,128)}, f32[1,1024]{1,0:T(1,128)S(1)}, u32[]{:S(2)}) copy-start(f32[1,1024]{1,0:T(1,128)S(1)} %get-tuple-element.72) | copy-start | bytes 12292
  18.0 13.2 %copy-start.29 = (f32[1,1024]{1,0:T(1,128)}, f32[1,1024]{1,0:T(1,128)S(1)}, u32[]{:S(2)}) copy-start(f32[1,1024]{1,0:T(1,128)S(1)} %get-tuple-element.73) | copy-start | bytes 12292
  18.9 12.2 %copy-start.31 = (s32[256]{0:T(256)}, s32[256]{0:T(256)S(1)}, u32[]{:S(2)}) copy-start(s32[256]{0:T(256)S(1)} %fusion.161) | copy-start | bytes 3076
  19.7 16.2 %copy-start.34 = (s32[128]{0:T(128)}, s32[128]{0:T(128)S(1)}, u32[]{:S(2)}) copy-start(s32[128]{0:T(128)S(1)} %get-tuple-element.86) | copy-start | bytes 1540
  19.7 16.2 %copy-start.36 = (s32[128]{0:T(128)}, s32[128]{0:T(128)S(1)}, u32[]{:S(2)}) copy-start(s32[128]{0:T(128)S(1)} %get-tuple-element.87) | copy-start | bytes 1540
  94.0 92.6 %copy-start.47 = (bf16[1,1024,512]{2,1,0:T(8,128)(2,1)S(1)}, bf16[1,1024,512]{2,1,0:T(8,128)(2,1)}, u32[]{:S(2)}) copy-start(bf16[1,1024,512]{2,1,0:T(8,128)(2,1)} %param.13) | copy-start | bytes 3145732
  94.0 92.5 %all-gather.14.cloned.1.call-start = ((), (), s32[]{:S(2)}) async-start(), calls=%async_computation.7 | async-start | bytes 12582912 | tf_op jit(solution)/shard_map/all_gather | solution.py:126
  157.7 89.8 %reduce-scatter.3.cloned.1.call-start = ((), (), s32[]{:S(2)}) async-start(), calls=%async_computation.4 | async-start | bytes 12582912 | tf_op jit(solution)/shard_map/reduce_scatter | solution.py:156
  186.5 4.7 copy-start.46
  224.3 85.6 %reduce-scatter.5.cloned.1.call-start = ((), (), s32[]{:S(2)}) async-start(), calls=%async_computation.5 | async-start | bytes 6291456 | tf_op jit(solution)/shard_map/reduce_scatter | solution.py:157
  247.4 72.3 %copy-start.32 = (s32[256]{0:T(256)S(1)}, s32[256]{0:T(256)}, u32[]{:S(2)}) copy-start(s32[256]{0:T(256)} %copy-done.31) | copy-start | bytes 3076
  247.4 72.5 %copy-start.33 = (s32[1,128,2]{1,2,0:T(2,128)S(1)}, s32[1,128,2]{1,2,0:T(2,128)}, u32[]{:S(2)}) copy-start(s32[1,128,2]{1,2,0:T(2,128)} %param.12) | copy-start | bytes 3076
  309.9 58.0 %all-to-all-start.1 = ((bf16[32,16,2048]{2,1,0:T(8,128)(2,1)}), bf16[32,16,2048]{2,1,0:T(8,128)(2,1)S(1)}, u32[]{:S(2)}, u32[]{:S(2)}) async-start(bf16[32,16,2048]{2,1,0:T(8,128)(2,1)} %bitcast.187), calls=%async_computation.3 | async-start | bytes 4194304 | tf_op jit(solution)/shard_map/all_to_all | solution.py:159
  319.5 94.4 %all-gather.16.cloned.1.call-start = ((), (), s32[]{:S(2)}) async-start(), calls=%async_computation.8 | async-start | bytes 1310720 | tf_op jit(solution)/shard_map/all_gather | solution.py:185
  370.3 4.9 copy-start.45
  370.3 4.9 copy-start.4
  391.5 84.6 %all-gather.18.cloned.1.call-start = ((), (), s32[]{:S(2)}) async-start(), calls=%async_computation.9 | async-start | bytes 2359296 | tf_op jit(solution)/shard_map/all_gather | solution.py:185
  415.9 9.7 %copy-start.50 = (bf16[2048,512]{1,0:T(8,128)(2,1)S(1)}, bf16[2048,512]{1,0:T(8,128)(2,1)}, u32[]{:S(2)}) copy-start(bf16[2048,512]{1,0:T(8,128)(2,1)} %copy-done.49) | copy-start | bytes 6291460
  422.9 23.8 %collective-permute-start.5 = (bf16[512,1024]{1,0:T(8,128)(2,1)}, bf16[512,1024]{1,0:T(8,128)(2,1)}, u32[]{:S(2)}, u32[]{:S(2)}) collective-permute-start(bf16[512,1024]{1,0:T(8,128)(2,1)} %fusion.11), channel_id=1, source_target_pairs={{0,1},{1,0},{2,3},{3,2},{4,5},{5,4},{6,7},{7,6},{8,9},{9,8},{10,11... | collective-permute-start | bytes 3145736 | tf_op jit(solution)/shard_map/ppermute | solution.py:147
  430.1 39.0 %collective-permute-start.4 = (bf16[1024,512]{1,0:T(8,128)(2,1)S(1)}, bf16[1024,512]{1,0:T(8,128)(2,1)}, u32[]{:S(2)}, u32[]{:S(2)}) collective-permute-start(bf16[1024,512]{1,0:T(8,128)(2,1)S(1)} %fusion.8), channel_id=1, source_target_pairs={{0,1},{1,0},{2,3},{3,2},{4,5},{5,4},{6,7},{7,6},{8,9},{9,8},{10,11... | collective-permute-start | bytes 3145736 | tf_op jit(solution)/shard_map/ppermute | solution.py:146
  430.5 42.7 %copy-start.10 = (f32[1,1024]{1,0:T(1,128)S(1)}, f32[1,1024]{1,0:T(1,128)}, u32[]{:S(2)}) copy-start(f32[1,1024]{1,0:T(1,128)} %copy-done.9) | copy-start | bytes 12292
  430.5 42.7 %copy-start.12 = (f32[1,1024]{1,0:T(1,128)S(1)}, f32[1,1024]{1,0:T(1,128)}, u32[]{:S(2)}) copy-start(f32[1,1024]{1,0:T(1,128)} %copy-done.11) | copy-start | bytes 12292
  430.5 42.7 %copy-start.14 = (f32[1,1024]{1,0:T(1,128)S(1)}, f32[1,1024]{1,0:T(1,128)}, u32[]{:S(2)}) copy-start(f32[1,1024]{1,0:T(1,128)} %copy-done.13) | copy-start | bytes 12292
  430.5 42.7 %copy-start.16 = (f32[1,1024]{1,0:T(1,128)S(1)}, f32[1,1024]{1,0:T(1,128)}, u32[]{:S(2)}) copy-start(f32[1,1024]{1,0:T(1,128)} %copy-done.15) | copy-start | bytes 12292
  430.5 42.7 %copy-start.18 = (f32[1,1024]{1,0:T(1,128)S(1)}, f32[1,1024]{1,0:T(1,128)}, u32[]{:S(2)}) copy-start(f32[1,1024]{1,0:T(1,128)} %copy-done.17) | copy-start | bytes 12292
  430.5 42.7 %copy-start.20 = (f32[1,1024]{1,0:T(1,128)S(1)}, f32[1,1024]{1,0:T(1,128)}, u32[]{:S(2)}) copy-start(f32[1,1024]{1,0:T(1,128)} %copy-done.19) | copy-start | bytes 12292
  430.5 42.7 %copy-start.22 = (f32[1,1024]{1,0:T(1,128)S(1)}, f32[1,1024]{1,0:T(1,128)}, u32[]{:S(2)}) copy-start(f32[1,1024]{1,0:T(1,128)} %copy-done.21) | copy-start | bytes 12292
  430.5 42.7 %copy-start.24 = (f32[1,1024]{1,0:T(1,128)S(1)}, f32[1,1024]{1,0:T(1,128)}, u32[]{:S(2)}) copy-start(f32[1,1024]{1,0:T(1,128)} %copy-done.23) | copy-start | bytes 12292
  430.5 42.7 %copy-start.26 = (f32[1,1024]{1,0:T(1,128)S(1)}, f32[1,1024]{1,0:T(1,128)}, u32[]{:S(2)}) copy-start(f32[1,1024]{1,0:T(1,128)} %copy-done.25) | copy-start | bytes 12292
  430.6 42.7 %copy-start.28 = (f32[1,1024]{1,0:T(1,128)S(1)}, f32[1,1024]{1,0:T(1,128)}, u32[]{:S(2)}) copy-start(f32[1,1024]{1,0:T(1,128)} %copy-done.27) | copy-start | bytes 12292
  430.6 42.7 %copy-start.30 = (f32[1,1024]{1,0:T(1,128)S(1)}, f32[1,1024]{1,0:T(1,128)}, u32[]{:S(2)}) copy-start(f32[1,1024]{1,0:T(1,128)} %copy-done.29) | copy-start | bytes 12292
  450.0 22.1 %collective-permute-start.2 = (bf16[15,1024]{1,0:T(8,128)(2,1)S(1)}, bf16[15,1024]{1,0:T(8,128)(2,1)S(1)}, u32[]{:S(2)}, u32[]{:S(2)}) collective-permute-start(bf16[15,1024]{1,0:T(8,128)(2,1)S(1)} %get-tuple-element.49), channel_id=1, source_target_pairs={{0,2},{2,4},{4,6},{6,8},{8,10},{10,12},{12,14},{14,16},{16,18},{18... | collective-permute-start | bytes 92168 | tf_op jit(solution)/shard_map/ppermute | solution.py:19
  459.8 13.3 %collective-permute-start.3 = (bf16[15,1024]{1,0:T(8,128)(2,1)S(1)}, bf16[15,1024]{1,0:T(8,128)(2,1)S(1)}, u32[]{:S(2)}, u32[]{:S(2)}) collective-permute-start(bf16[15,1024]{1,0:T(8,128)(2,1)S(1)} %get-tuple-element.50), channel_id=1, source_target_pairs={{2,0},{4,2},{6,4},{8,6},{10,8},{12,10},{14,12},{16,14},{18,16},{20... | collective-permute-start | bytes 92168 | tf_op jit(solution)/shard_map/ppermute | solution.py:20
  473.3 13.9 %copy-start.1 = (bf16[1,512,1024]{2,1,0:T(8,128)(2,1)S(1)}, bf16[1,512,1024]{2,1,0:T(8,128)(2,1)}, u32[]{:S(2)}) copy-start(bf16[1,512,1024]{2,1,0:T(8,128)(2,1)} %param.14) | copy-start | bytes 3145732
  (16 other events, 49.6 us)
Sparse Core Ops, SparseCore 0:
  94.1 63.4 all-gather.11
  159.4 27.0 all-gather.13
  224.5 22.9 reduce-scatter.2
  249.8 60.0 reduce-scatter.4
  391.6 22.2 all-gather.15
  416.0 39.1 all-gather.17
